TPU v7x, 512 devices: a whole 4x8x8 slice. The times are simulated.
512 devices in a mesh: ctx: 32 (over z, x), exp: 16 (over y, core).
Axes of the slice: x: 4, y: 8, z: 8, core: 2. Of those that a mesh axis runs over, the one named last changes fastest.
Arguments:
- stream: bfloat16 [16, 4096, 1024], P('exp', 'ctx'), may hold values from -400 to 400
- queries: bfloat16 [16, 4096, 16, 128], P('exp', 'ctx'), may hold values from -6 to 6
- key_rows: bfloat16 [16, 4096, 2, 128], P('exp', 'ctx'), may hold values from -4 to 4
- value_rows: bfloat16 [16, 4096, 2, 128], P('exp', 'ctx'), may hold values from -6 to 6
- expert_ids: int32 [16, 4096, 2], P('exp', 'ctx'), may hold values from 0 to 127, as said below
- norm_gain: bfloat16 [1024], replicated, may hold values from 0.099609375 to 1.8984375
- router_weight: bfloat16 [1024, 128], replicated, may hold values from -0.1875 to 0.1875
- gate_weight: bfloat16 [98304, 1024], P(('ctx', 'exp')), may hold values from -0.1875 to 0.1875
- up_weight: bfloat16 [98304, 1024], P(('ctx', 'exp')), may hold values from -0.1875 to 0.1875
- down_weight: bfloat16 [98304, 1024], P(('ctx', 'exp')), may hold values from -0.21875 to 0.21875
Outputs:
- attended: bfloat16 [16, 4096, 16, 128], P('exp', 'ctx')
- expert_mix: bfloat16 [16, 4096, 1024], P('exp', 'ctx')
Inputs may be any that keep to these rules, and one draw needn't show every extreme that they name: `expert_ids`: within the rows of one device (aligned blocks of 128 positions of one sequence), a token's 2 experts differ and no expert is named more than 4 times; one expert is named exactly 4 times in every such block.
All inputs are finite; a program needn't handle non-finite values.
Results may differ from a plain program's by a relative error of at most 0.01.
Values may be sent and summed in bfloat16 or wider, within the bound.
No kernel may reach another device: no remote copies, remote signals or barrier semaphores. Data moves between devices by JAX's collectives and lax.ppermute only.
A program may use at most 64 MiB of HBM per device.

v0:
```python
import math
import jax
import jax.numpy as jnp
from jax import lax
from jax.sharding import PartitionSpec as P


def from_partner(value, axis, bit):
    return lax.ppermute(value, axis, [(i, i ^ 1 << bit) for i in range(lax.axis_size(axis))])


def expert_rows(inputs, gate_rows, up_rows, down_rows):
    features = inputs.shape[-1]
    flat_rows = inputs.reshape(-1, features)
    contract = (((1,), (1,)), ((), ()))
    gate_part = lax.dot_general(flat_rows, gate_rows, contract, preferred_element_type=jnp.float32)
    up_part = lax.dot_general(flat_rows, up_rows, contract, preferred_element_type=jnp.float32)
    hidden = (jax.nn.silu(gate_part) * up_part).astype(jnp.bfloat16)
    projected = jnp.dot(hidden, down_rows, preferred_element_type=jnp.float32)
    return projected.reshape(inputs.shape)


def attention(queries, key_rows, value_rows):
    seq_rows = queries.shape[1]
    head_count = queries.shape[2]
    head_size = queries.shape[3]
    kv_count = key_rows.shape[2]
    group_size = head_count // kv_count
    grouped = queries[0].reshape(seq_rows, kv_count, group_size, head_size)
    scaling = 1.0 / math.sqrt(head_size)
    query_pos = lax.axis_index("ctx") * seq_rows + jnp.arange(seq_rows, dtype=jnp.int32)
    initial = (
        jnp.full((kv_count, group_size, seq_rows), -1e30, jnp.float32),
        jnp.zeros((kv_count, group_size, seq_rows), jnp.float32),
        jnp.zeros((kv_count, group_size, seq_rows, head_size), jnp.float32),
    )
    key_piece = lax.all_gather(key_rows, "ctx", axis=1, tiled=True)
    value_piece = lax.all_gather(value_rows, "ctx", axis=1, tiled=True)
    piece_rows = key_piece.shape[1]
    block_rows = math.gcd(piece_rows, 512)
    block_count = piece_rows // block_rows
    key_blocks = key_piece[0].reshape(block_count, block_rows, kv_count, head_size)
    value_blocks = value_piece[0].reshape(block_count, block_rows, kv_count, head_size)

    def advance(status, members):
        running, totals, accumulated = status
        key_block, value_block, offset = members
        scores = (
            jnp.einsum("qhgd,khd->hgqk", grouped, key_block, preferred_element_type=jnp.float32)
            * scaling
        )
        key_pos = offset * block_rows + jnp.arange(block_rows, dtype=jnp.int32)
        visible = key_pos[None, :] <= query_pos[:, None]
        scores = jnp.where(visible, scores, -1e30)
        highest = jnp.maximum(running, jnp.max(scores, axis=-1))
        factor = jnp.exp(running - highest)
        weights = jnp.where(visible, jnp.exp(scores - highest[..., None]), 0.0)
        totals = totals * factor + jnp.sum(weights, axis=-1)
        accumulated = accumulated * factor[..., None] + jnp.einsum(
            "hgqk,khd->hgqd",
            weights.astype(jnp.bfloat16),
            value_block,
            preferred_element_type=jnp.float32,
        )
        return ((highest, totals, accumulated), None)

    status, unused = lax.scan(
        advance, initial, (key_blocks, value_blocks, jnp.arange(block_count, dtype=jnp.int32))
    )
    running, totals, accumulated = status
    result = accumulated / totals[..., None]
    return (
        jnp.transpose(result, (2, 0, 1, 3))
        .reshape(1, seq_rows, head_count, head_size)
        .astype(jnp.bfloat16)
    )


def local(
    stream,
    queries,
    key_rows,
    value_rows,
    expert_ids,
    norm_gain,
    router_weight,
    gate_weight,
    up_weight,
    down_weight,
):
    attended = attention(queries, key_rows, value_rows)
    ctx_count = lax.axis_size("ctx")
    exp_count = lax.axis_size("exp")
    tokens = stream.shape[1]
    features = stream.shape[2]
    top_count = expert_ids.shape[2]
    expert_total = router_weight.shape[1]
    per_ctx = expert_total // ctx_count
    quarters = exp_count // per_ctx
    capacity = 2 * tokens * top_count // expert_total
    widened = stream[0].astype(jnp.float32)
    mean_square = jnp.mean(widened * widened, axis=-1, keepdims=True)
    normed = (widened * lax.rsqrt(mean_square + 1e-06) * norm_gain.astype(jnp.float32)).astype(
        jnp.bfloat16
    )
    logits = jnp.dot(normed, router_weight, preferred_element_type=jnp.float32)
    chosen = expert_ids[0]
    gate_values = jax.nn.sigmoid(jnp.take_along_axis(logits, chosen, axis=1))
    flat_ids = chosen.reshape(-1)
    onehot = (flat_ids[:, None] == jnp.arange(expert_total, dtype=jnp.int32)[None, :]).astype(
        jnp.int32
    )
    earlier = jnp.cumsum(onehot, axis=0) - onehot
    slot_index = jnp.sum(earlier * onehot, axis=1)
    target = (flat_ids % per_ctx * ctx_count + flat_ids // per_ctx) * capacity + slot_index
    source_rows = jnp.repeat(normed, top_count, axis=0)
    outgoing = (
        jnp.zeros((expert_total * capacity, features), jnp.bfloat16).at[target].set(source_rows)
    )
    outgoing = outgoing.reshape(per_ctx, ctx_count, capacity, features)
    arrived = lax.all_to_all(outgoing, "ctx", split_axis=1, concat_axis=1, tiled=True)
    stacked = jnp.stack([gate_weight, up_weight, down_weight], axis=0)
    my_exp = lax.axis_index("exp")
    partner = from_partner(stacked, "exp", 0)
    upper_side = my_exp & 1 == 1
    held = jnp.where(
        upper_side,
        jnp.concatenate([partner, stacked], axis=1),
        jnp.concatenate([stacked, partner], axis=1),
    )
    half_ctx = ctx_count // 2
    halves_rows = arrived.reshape(per_ctx, 1, 2, half_ctx, capacity, features)
    spread_rows = jnp.broadcast_to(
        halves_rows, (per_ctx, quarters // 2, 2, half_ctx, capacity, features)
    )
    spread_rows = spread_rows.reshape(exp_count, half_ctx, capacity, features)
    received = lax.all_to_all(spread_rows, "exp", split_axis=0, concat_axis=0, tiled=True)
    partials = expert_rows(received, held[0], held[1], held[2])
    returned = lax.all_to_all(
        partials.astype(jnp.bfloat16), "exp", split_axis=0, concat_axis=0, tiled=True
    ).astype(partials.dtype)
    summed = jnp.sum(
        returned.reshape(per_ctx, quarters // 2, 2, half_ctx, capacity, features), axis=1
    )
    finished = summed.astype(jnp.bfloat16).reshape(per_ctx, ctx_count, capacity, features)
    came_back = lax.all_to_all(finished, "ctx", split_axis=1, concat_axis=1, tiled=True)
    flat_back = came_back.reshape(expert_total * capacity, features)
    picked = (
        jnp.take(flat_back, target, axis=0).astype(jnp.float32).reshape(tokens, top_count, features)
    )
    mixture = jnp.sum(picked * gate_values[:, :, None], axis=1).astype(jnp.bfloat16)
    return (attended, mixture[None])


def solution(mesh):
    placed = (
        P("exp", "ctx", None),
        P("exp", "ctx", None, None),
        P("exp", "ctx", None, None),
        P("exp", "ctx", None, None),
        P("exp", "ctx", None),
        P(),
        P(),
        P(("ctx", "exp"), None),
        P(("ctx", "exp"), None),
        P(("ctx", "exp"), None),
    )
    return jax.shard_map(
        local,
        mesh=mesh,
        in_specs=placed,
        out_specs=(P("exp", "ctx", None, None), P("exp", "ctx", None)),
        check_vma=False,
    )
```

profile of v0, /device:TPU:16, one launch (start us, length us, event | category | flops | bytes accessed | tf_op | source)
XLA Modules:
  0.0 309.8 jit_solution(2212090198150793443)
XLA Ops:
  12.4 1.9 scatter_custom_fusion
  16.4 13.2 %all-to-all-start = ((bf16[4,32,4,1024]{3,2,0,1:T(4,128)(2,1)}), bf16[4,32,4,1024]{3,2,0,1:T(4,128)(2,1)S(1)}, u32[]{:S(2)}, u32[]{:S(2)}) async-start(bf16[4,32,4,1024]{3,2,0,1:T(4,128)(2,1)} %copy.84), calls=%async_computation | async-start | bytes 2097152 | tf_op jit(solution)/shard_map/all_to_all | solution.py:121
  30.3 27.4 %all-to-all-done = bf16[4,32,4,1024]{3,2,0,1:T(4,128)(2,1)S(1)} async-done(((bf16[4,32,4,1024]{3,2,0,1:T(4,128)(2,1)}), bf16[4,32,4,1024]{3,2,0,1:T(4,128)(2,1)S(1)}, u32[]{:S(2)}, u32[]{:S(2)}) %all-to-all-start) | async-done | bytes 1048608 | tf_op jit(solution)/shard_map/all_to_all | solution.py:121
  58.1 2.1 broadcast_in_dim.66
  60.2 7.6 %all-to-all-start.1 = ((bf16[16,16,4,1024]{3,2,1,0:T(4,128)(2,1)}), bf16[16,16,4,1024]{3,2,1,0:T(4,128)(2,1)S(1)}, u32[]{:S(2)}, u32[]{:S(2)}) async-start(bf16[16,16,4,1024]{3,2,1,0:T(4,128)(2,1)} %bitcast.120), calls=%async_computation.1 | async-start | bytes 4194304 | tf_op jit(solution)/shard_map/all_to_all | solution.py:137
  67.8 2.2 pad_maximum_fusion
  70.0 2.0 collective-permute-start
  72.7 2.3 collective-permute-done
  75.1 3.5 %maximum_select_fusion = bf16[3,384,1024]{2,1,0:T(8,128)(2,1)} fusion(bf16[1,192,1024]{2,1,0:T(8,128)(2,1)S(1)} %bitcast.124, bf16[1,192,1024]{2,1,0:T(8,128)(2,1)S(1)} %bitcast.126, bf16[1,192,1024]{2,1,0:T(8,128)(2,1)} %bitcast.128, bf16[3,192,1024]{2,1,0:T(8,128)(2,1)} %collective-permute-done, pred[]{:T(512)S(6)} %eq.35), kind=kLoop, calls=%fused_computation.30 | loop fusion | flops 20054016 | bytes 4718593 | tf_op jit(solution)/shard_map/jit(_where)/select_n | solution.py:126
  78.6 36.6 %all-to-all-done.1 = bf16[16,16,4,1024]{3,2,1,0:T(4,128)(2,1)S(1)} async-done(((bf16[16,16,4,1024]{3,2,1,0:T(4,128)(2,1)}), bf16[16,16,4,1024]{3,2,1,0:T(4,128)(2,1)S(1)}, u32[]{:S(2)}, u32[]{:S(2)}) %all-to-all-start.1) | async-done | bytes 2097184 | tf_op jit(solution)/shard_map/all_to_all | solution.py:137
  115.2 2.0 reshape.284
  117.2 3.2 %fusion.22 = f32[1024,384]{1,0:T(8,128)S(1)} fusion(bf16[1024,1024]{1,0:T(8,128)(2,1)} %reshape.284, bf16[3,384,1024]{2,1,0:T(8,128)(2,1)} %maximum_select_fusion), kind=kOutput, calls=%fused_computation.40 | convolution fusion | flops 805306368 | bytes 4456448 | tf_op jit(solution)/shard_map/dot_general | solution.py:16
  120.4 2.3 multiply_convert_fusion
  122.7 2.4 dot_general.22
  125.1 3.7 %convolution_convert_fusion = bf16[16,16,4,1024]{3,1,2,0:T(8,128)(2,1)} fusion(bf16[3,384,1024]{2,1,0:T(8,128)(2,1)S(1)} %copy-done.2, bf16[16,16,4,384]{3,2,1,0:T(4,128)(2,1)} %dot_general.22), kind=kOutput, calls=%fused_computation.31 | convolution fusion | flops 806354944 | bytes 3670016 | tf_op jit(solution)/shard_map/dot_general | solution.py:19
  128.8 6.7 %all-to-all-start.2 = ((bf16[16,16,4,1024]{3,1,2,0:T(8,128)(2,1)}), bf16[16,16,4,1024]{3,1,2,0:T(8,128)(2,1)S(1)}, u32[]{:S(2)}, u32[]{:S(2)}) async-start(bf16[16,16,4,1024]{3,1,2,0:T(8,128)(2,1)} %convolution_convert_fusion), calls=%async_computation.2 | async-start | bytes 4194304 | tf_op jit(solution)/shard_map/all_to_all | solution.py:139
  137.6 1.9 gather_fusion.1
  139.9 43.0 %all-to-all-done.2 = bf16[16,16,4,1024]{3,1,2,0:T(8,128)(2,1)S(1)} async-done(((bf16[16,16,4,1024]{3,1,2,0:T(8,128)(2,1)}), bf16[16,16,4,1024]{3,1,2,0:T(8,128)(2,1)S(1)}, u32[]{:S(2)}, u32[]{:S(2)}) %all-to-all-start.2) | async-done | bytes 2097184 | tf_op jit(solution)/shard_map/all_to_all | solution.py:139
  182.8 1.8 reduce
  185.9 1.8 copy.88
  187.7 5.3 %all-to-all-start.3 = ((bf16[4,32,4,1024]{3,2,0,1:T(4,128)(2,1)}), bf16[4,32,4,1024]{3,2,0,1:T(4,128)(2,1)S(1)}, u32[]{:S(2)}, u32[]{:S(2)}) async-start(bf16[4,32,4,1024]{3,2,0,1:T(4,128)(2,1)} %copy.88), calls=%async_computation.3 | async-start | bytes 2097152 | tf_op jit(solution)/shard_map/all_to_all | solution.py:146
  193.1 14.3 %all-gather.5.cloned.1.call-done = bf16[1,4096,2,128]{3,1,2,0:T(8,128)(2,1)} async-done(((bf16[1,128,2,128]{3,1,2,0:T(8,128)(2,1)}), bf16[1,4096,2,128]{3,1,2,0:T(8,128)(2,1)}) %all-gather.5.cloned.1.call-update) | async-done | bytes 2097168 | tf_op jit(solution)/shard_map/all_gather | solution.py:38
  207.4 89.6 %while.15 = (s32[]{:T(128)}, f32[2,8,128]{2,1,0:T(8,128)S(1)}, f32[2,8,128]{2,1,0:T(8,128)S(1)}, f32[2,8,128,128]{3,2,1,0:T(8,128)S(1)}, s32[8]{0:T(128)S(1)}, /...) while((s32[]{:T(128)}, f32[2,8,128]{2,1,0:T(8,128)S(1)}, ...), condition=%wide.region_3.4_spmd.clone, body=%wide.region_0.3_spmd.clone.sunk | while | flops 551365248 | bytes 32904396 | solution.py:67
  208.8 3.7 %fusion.58 = (f32[2,8,128]{2,1,0:T(8,128)S(1)}, f32[2,512,128,8]{2,1,3,0:T(8,128)}) fusion(pred[128,512]{0,1:T(8,128)(4,1)S(1)} %broadcast_compare_fusion.2, bf16[128,2,8,128]{3,0,2,1:T(8,128)(2,1)S(1)} %get-tuple-element.236, bf16[8,512,2,128]{3,1,0,2:T(8,128)(2,1)} %get-tuple-element.235, s32[]{:T(128)S(6)} %copy.107), kind=kOutput, calls=%fused_computation.6.clone.1 | convolution fusion | flops 271579136 | bytes 5054468 | tf_op jit(solution)/shard_map/while/body/eval_jaxpr/qhgd,khd->hgqk/dot_general | solution.py:49
  212.5 3.3 %fusion.59 = f32[2,8,128]{2,1,0:T(8,128)S(1)} fusion(f32[2,512,128,8]{2,1,3,0:T(8,128)} %get-tuple-element.203, f32[2,8,128]{2,1,0:T(8,128)S(1)} %select_maximum_fusion.2, pred[128,512]{0,1:T(8,128)(4,1)S(1)} %broadcast_compare_fusion.2), kind=kLoop, calls=%fused_computation.8.clone.1 | loop fusion | flops 5240832 | bytes 4276224 | tf_op jit(solution)/shard_map/while/body/eval_jaxpr/reduce_sum | solution.py:58
  216.0 2.6 fusion.61
  220.0 3.7 %fusion.58 = (f32[2,8,128]{2,1,0:T(8,128)S(1)}, f32[2,512,128,8]{2,1,3,0:T(8,128)}) fusion(pred[128,512]{0,1:T(8,128)(4,1)S(1)} %broadcast_compare_fusion.2, bf16[128,2,8,128]{3,0,2,1:T(8,128)(2,1)S(1)} %get-tuple-element.236, bf16[8,512,2,128]{3,1,0,2:T(8,128)(2,1)} %get-tuple-element.235, s32[]{:T(128)S(6)} %copy.107), kind=kOutput, calls=%fused_computation.6.clone.1 | convolution fusion | flops 271579136 | bytes 5054468 | tf_op jit(solution)/shard_map/while/body/eval_jaxpr/qhgd,khd->hgqk/dot_general | solution.py:49
  223.7 3.3 %fusion.59 = f32[2,8,128]{2,1,0:T(8,128)S(1)} fusion(f32[2,512,128,8]{2,1,3,0:T(8,128)} %get-tuple-element.203, f32[2,8,128]{2,1,0:T(8,128)S(1)} %select_maximum_fusion.2, pred[128,512]{0,1:T(8,128)(4,1)S(1)} %broadcast_compare_fusion.2), kind=kLoop, calls=%fused_computation.8.clone.1 | loop fusion | flops 5240832 | bytes 4276224 | tf_op jit(solution)/shard_map/while/body/eval_jaxpr/reduce_sum | solution.py:58
  227.2 2.6 fusion.61
  231.2 3.7 %fusion.58 = (f32[2,8,128]{2,1,0:T(8,128)S(1)}, f32[2,512,128,8]{2,1,3,0:T(8,128)}) fusion(pred[128,512]{0,1:T(8,128)(4,1)S(1)} %broadcast_compare_fusion.2, bf16[128,2,8,128]{3,0,2,1:T(8,128)(2,1)S(1)} %get-tuple-element.236, bf16[8,512,2,128]{3,1,0,2:T(8,128)(2,1)} %get-tuple-element.235, s32[]{:T(128)S(6)} %copy.107), kind=kOutput, calls=%fused_computation.6.clone.1 | convolution fusion | flops 271579136 | bytes 5054468 | tf_op jit(solution)/shard_map/while/body/eval_jaxpr/qhgd,khd->hgqk/dot_general | solution.py:49
  234.9 3.3 %fusion.59 = f32[2,8,128]{2,1,0:T(8,128)S(1)} fusion(f32[2,512,128,8]{2,1,3,0:T(8,128)} %get-tuple-element.203, f32[2,8,128]{2,1,0:T(8,128)S(1)} %select_maximum_fusion.2, pred[128,512]{0,1:T(8,128)(4,1)S(1)} %broadcast_compare_fusion.2), kind=kLoop, calls=%fused_computation.8.clone.1 | loop fusion | flops 5240832 | bytes 4276224 | tf_op jit(solution)/shard_map/while/body/eval_jaxpr/reduce_sum | solution.py:58
  238.4 2.6 fusion.61
  242.5 3.7 %fusion.58 = (f32[2,8,128]{2,1,0:T(8,128)S(1)}, f32[2,512,128,8]{2,1,3,0:T(8,128)}) fusion(pred[128,512]{0,1:T(8,128)(4,1)S(1)} %broadcast_compare_fusion.2, bf16[128,2,8,128]{3,0,2,1:T(8,128)(2,1)S(1)} %get-tuple-element.236, bf16[8,512,2,128]{3,1,0,2:T(8,128)(2,1)} %get-tuple-element.235, s32[]{:T(128)S(6)} %copy.107), kind=kOutput, calls=%fused_computation.6.clone.1 | convolution fusion | flops 271579136 | bytes 5054468 | tf_op jit(solution)/shard_map/while/body/eval_jaxpr/qhgd,khd->hgqk/dot_general | solution.py:49
  246.1 3.3 %fusion.59 = f32[2,8,128]{2,1,0:T(8,128)S(1)} fusion(f32[2,512,128,8]{2,1,3,0:T(8,128)} %get-tuple-element.203, f32[2,8,128]{2,1,0:T(8,128)S(1)} %select_maximum_fusion.2, pred[128,512]{0,1:T(8,128)(4,1)S(1)} %broadcast_compare_fusion.2), kind=kLoop, calls=%fused_computation.8.clone.1 | loop fusion | flops 5240832 | bytes 4276224 | tf_op jit(solution)/shard_map/while/body/eval_jaxpr/reduce_sum | solution.py:58
  249.6 2.6 fusion.61
  253.7 3.7 %fusion.58 = (f32[2,8,128]{2,1,0:T(8,128)S(1)}, f32[2,512,128,8]{2,1,3,0:T(8,128)}) fusion(pred[128,512]{0,1:T(8,128)(4,1)S(1)} %broadcast_compare_fusion.2, bf16[128,2,8,128]{3,0,2,1:T(8,128)(2,1)S(1)} %get-tuple-element.236, bf16[8,512,2,128]{3,1,0,2:T(8,128)(2,1)} %get-tuple-element.235, s32[]{:T(128)S(6)} %copy.107), kind=kOutput, calls=%fused_computation.6.clone.1 | convolution fusion | flops 271579136 | bytes 5054468 | tf_op jit(solution)/shard_map/while/body/eval_jaxpr/qhgd,khd->hgqk/dot_general | solution.py:49
  257.3 3.3 %fusion.59 = f32[2,8,128]{2,1,0:T(8,128)S(1)} fusion(f32[2,512,128,8]{2,1,3,0:T(8,128)} %get-tuple-element.203, f32[2,8,128]{2,1,0:T(8,128)S(1)} %select_maximum_fusion.2, pred[128,512]{0,1:T(8,128)(4,1)S(1)} %broadcast_compare_fusion.2), kind=kLoop, calls=%fused_computation.8.clone.1 | loop fusion | flops 5240832 | bytes 4276224 | tf_op jit(solution)/shard_map/while/body/eval_jaxpr/reduce_sum | solution.py:58
  260.8 2.6 fusion.61
  264.9 3.7 %fusion.58 = (f32[2,8,128]{2,1,0:T(8,128)S(1)}, f32[2,512,128,8]{2,1,3,0:T(8,128)}) fusion(pred[128,512]{0,1:T(8,128)(4,1)S(1)} %broadcast_compare_fusion.2, bf16[128,2,8,128]{3,0,2,1:T(8,128)(2,1)S(1)} %get-tuple-element.236, bf16[8,512,2,128]{3,1,0,2:T(8,128)(2,1)} %get-tuple-element.235, s32[]{:T(128)S(6)} %copy.107), kind=kOutput, calls=%fused_computation.6.clone.1 | convolution fusion | flops 271579136 | bytes 5054468 | tf_op jit(solution)/shard_map/while/body/eval_jaxpr/qhgd,khd->hgqk/dot_general | solution.py:49
  268.6 3.3 %fusion.59 = f32[2,8,128]{2,1,0:T(8,128)S(1)} fusion(f32[2,512,128,8]{2,1,3,0:T(8,128)} %get-tuple-element.203, f32[2,8,128]{2,1,0:T(8,128)S(1)} %select_maximum_fusion.2, pred[128,512]{0,1:T(8,128)(4,1)S(1)} %broadcast_compare_fusion.2), kind=kLoop, calls=%fused_computation.8.clone.1 | loop fusion | flops 5240832 | bytes 4276224 | tf_op jit(solution)/shard_map/while/body/eval_jaxpr/reduce_sum | solution.py:58
  272.0 2.6 fusion.61
  276.1 3.7 %fusion.58 = (f32[2,8,128]{2,1,0:T(8,128)S(1)}, f32[2,512,128,8]{2,1,3,0:T(8,128)}) fusion(pred[128,512]{0,1:T(8,128)(4,1)S(1)} %broadcast_compare_fusion.2, bf16[128,2,8,128]{3,0,2,1:T(8,128)(2,1)S(1)} %get-tuple-element.236, bf16[8,512,2,128]{3,1,0,2:T(8,128)(2,1)} %get-tuple-element.235, s32[]{:T(128)S(6)} %copy.107), kind=kOutput, calls=%fused_computation.6.clone.1 | convolution fusion | flops 271579136 | bytes 5054468 | tf_op jit(solution)/shard_map/while/body/eval_jaxpr/qhgd,khd->hgqk/dot_general | solution.py:49
  279.8 3.3 %fusion.59 = f32[2,8,128]{2,1,0:T(8,128)S(1)} fusion(f32[2,512,128,8]{2,1,3,0:T(8,128)} %get-tuple-element.203, f32[2,8,128]{2,1,0:T(8,128)S(1)} %select_maximum_fusion.2, pred[128,512]{0,1:T(8,128)(4,1)S(1)} %broadcast_compare_fusion.2), kind=kLoop, calls=%fused_computation.8.clone.1 | loop fusion | flops 5240832 | bytes 4276224 | tf_op jit(solution)/shard_map/while/body/eval_jaxpr/reduce_sum | solution.py:58
  283.2 2.6 fusion.61
  287.3 3.7 %fusion.58 = (f32[2,8,128]{2,1,0:T(8,128)S(1)}, f32[2,512,128,8]{2,1,3,0:T(8,128)}) fusion(pred[128,512]{0,1:T(8,128)(4,1)S(1)} %broadcast_compare_fusion.2, bf16[128,2,8,128]{3,0,2,1:T(8,128)(2,1)S(1)} %get-tuple-element.236, bf16[8,512,2,128]{3,1,0,2:T(8,128)(2,1)} %get-tuple-element.235, s32[]{:T(128)S(6)} %copy.107), kind=kOutput, calls=%fused_computation.6.clone.1 | convolution fusion | flops 271579136 | bytes 5054468 | tf_op jit(solution)/shard_map/while/body/eval_jaxpr/qhgd,khd->hgqk/dot_general | solution.py:49
  291.0 3.3 %fusion.59 = f32[2,8,128]{2,1,0:T(8,128)S(1)} fusion(f32[2,512,128,8]{2,1,3,0:T(8,128)} %get-tuple-element.203, f32[2,8,128]{2,1,0:T(8,128)S(1)} %select_maximum_fusion.2, pred[128,512]{0,1:T(8,128)(4,1)S(1)} %broadcast_compare_fusion.2), kind=kLoop, calls=%fused_computation.8.clone.1 | loop fusion | flops 5240832 | bytes 4276224 | tf_op jit(solution)/shard_map/while/body/eval_jaxpr/reduce_sum | solution.py:58
  294.4 2.6 fusion.61
  300.6 2.3 multiply_reduce_fusion
  (146 shorter events, 23.0 us)
Async XLA Ops:
  7.2 130.2 %copy-start = (bf16[1024,128]{1,0:T(8,128)(2,1)S(1)}, bf16[1024,128]{1,0:T(8,128)(2,1)}, u32[]{:S(2)}) copy-start(bf16[1024,128]{1,0:T(8,128)(2,1)} %param.18) | copy-start | bytes 786436
  14.8 14.8 %copy-start.7 = (bf16[1,128,2,128]{3,2,1,0:T(2,128)(2,1)S(1)}, bf16[1,128,2,128]{3,2,1,0:T(2,128)(2,1)}, u32[]{:S(2)}) copy-start(bf16[1,128,2,128]{3,2,1,0:T(2,128)(2,1)} %param.14) | copy-start | bytes 196612
  16.4 41.3 %all-to-all-start = ((bf16[4,32,4,1024]{3,2,0,1:T(4,128)(2,1)}), bf16[4,32,4,1024]{3,2,0,1:T(4,128)(2,1)S(1)}, u32[]{:S(2)}, u32[]{:S(2)}) async-start(bf16[4,32,4,1024]{3,2,0,1:T(4,128)(2,1)} %copy.84), calls=%async_computation | async-start | bytes 2097152 | tf_op jit(solution)/shard_map/all_to_all | solution.py:121
  29.5 163.6 %all-gather.3.cloned.1.call-start = ((), (), s32[]{:S(2)}) async-start(), calls=%async_computation.4 | async-start | bytes 2162688 | tf_op jit(solution)/shard_map/all_gather | solution.py:37
  60.2 7.6 %copy-start.4 = (bf16[192,1024]{1,0:T(8,128)(2,1)S(1)}, bf16[192,1024]{1,0:T(8,128)(2,1)}, u32[]{:S(2)}) copy-start(bf16[192,1024]{1,0:T(8,128)(2,1)} %param.21) | copy-start | bytes 1179652
  60.2 7.6 %copy-start.5 = (bf16[192,1024]{1,0:T(8,128)(2,1)S(1)}, bf16[192,1024]{1,0:T(8,128)(2,1)}, u32[]{:S(2)}) copy-start(bf16[192,1024]{1,0:T(8,128)(2,1)} %param.20) | copy-start | bytes 1179652
  60.2 11.9 %copy-start.8 = (bf16[1,128,2,128]{3,2,1,0:T(2,128)(2,1)S(1)}, bf16[1,128,2,128]{3,2,1,0:T(2,128)(2,1)}, u32[]{:S(2)}) copy-start(bf16[1,128,2,128]{3,2,1,0:T(2,128)(2,1)} %param.15) | copy-start | bytes 196612
  60.2 55.0 %all-to-all-start.1 = ((bf16[16,16,4,1024]{3,2,1,0:T(4,128)(2,1)}), bf16[16,16,4,1024]{3,2,1,0:T(4,128)(2,1)S(1)}, u32[]{:S(2)}, u32[]{:S(2)}) async-start(bf16[16,16,4,1024]{3,2,1,0:T(4,128)(2,1)} %bitcast.120), calls=%async_computation.1 | async-start | bytes 4194304 | tf_op jit(solution)/shard_map/all_to_all | solution.py:137
  67.8 139.7 %all-gather.5.cloned.1.call-start = ((), (), s32[]{:S(2)}) async-start(), calls=%async_computation.5 | async-start | bytes 2162688 | tf_op jit(solution)/shard_map/all_gather | solution.py:38
  70.0 5.1 %collective-permute-start = (bf16[3,192,1024]{2,1,0:T(8,128)(2,1)}, bf16[3,192,1024]{2,1,0:T(8,128)(2,1)}, u32[]{:S(2)}, u32[]{:S(2)}) collective-permute-start(bf16[3,192,1024]{2,1,0:T(8,128)(2,1)} %pad_maximum_fusion), channel_id=1, source_target_pairs={{0,1},{1,0},{2,3},{3,2},{4,5},{5,4},{6,7},{7,6},{8,9},{9,8},{10,11... | collective-permute-start | bytes 3538952 | tf_op jit(solution)/shard_map/ppermute | solution.py:9
  117.2 3.2 %copy-start.2 = (bf16[3,384,1024]{2,1,0:T(8,128)(2,1)S(1)}, bf16[3,384,1024]{2,1,0:T(8,128)(2,1)}, u32[]{:S(2)}) copy-start(bf16[3,384,1024]{2,1,0:T(8,128)(2,1)} %maximum_select_fusion) | copy-start | bytes 7077892
  117.2 3.2 %copy-start.3 = (bf16[1024,1024]{1,0:T(8,128)(2,1)S(1)}, bf16[1024,1024]{1,0:T(8,128)(2,1)}, u32[]{:S(2)}) copy-start(bf16[1024,1024]{1,0:T(8,128)(2,1)} %reshape.284) | copy-start | bytes 6291460
  128.8 8.1 %copy-start.9 = (s32[1,128,2]{1,2,0:T(2,128)S(1)}, s32[1,128,2]{1,2,0:T(2,128)}, u32[]{:S(2)}) copy-start(s32[1,128,2]{1,2,0:T(2,128)} %param.16) | copy-start | bytes 3076
  128.8 54.1 %all-to-all-start.2 = ((bf16[16,16,4,1024]{3,1,2,0:T(8,128)(2,1)}), bf16[16,16,4,1024]{3,1,2,0:T(8,128)(2,1)S(1)}, u32[]{:S(2)}, u32[]{:S(2)}) async-start(bf16[16,16,4,1024]{3,1,2,0:T(8,128)(2,1)} %convolution_convert_fusion), calls=%async_computation.2 | async-start | bytes 4194304 | tf_op jit(solution)/shard_map/all_to_all | solution.py:139
  185.9 21.5 %copy-start.6 = (f32[2,8,128,128]{3,2,1,0:T(8,128)S(1)}, f32[2,8,128,128]{3,2,1,0:T(8,128)}, u32[]{:S(2)}) copy-start(f32[2,8,128,128]{3,2,1,0:T(8,128)} %custom-call.4) | copy-start | bytes 3145732
  187.7 110.8 %all-to-all-start.3 = ((bf16[4,32,4,1024]{3,2,0,1:T(4,128)(2,1)}), bf16[4,32,4,1024]{3,2,0,1:T(4,128)(2,1)S(1)}, u32[]{:S(2)}, u32[]{:S(2)}) async-start(bf16[4,32,4,1024]{3,2,0,1:T(4,128)(2,1)} %copy.88), calls=%async_computation.3 | async-start | bytes 2097152 | tf_op jit(solution)/shard_map/all_to_all | solution.py:146
  212.5 3.4 %copy-start.1 = (f32[2,512,128,8]{2,1,3,0:T(8,128)S(1)}, f32[2,512,128,8]{2,1,3,0:T(8,128)}, u32[]{:S(2)}) copy-start(f32[2,512,128,8]{2,1,3,0:T(8,128)} %get-tuple-element.203) | copy-start | bytes 12582916 | tf_op jit(solution)/shard_map/while
  223.7 3.4 %copy-start.1 = (f32[2,512,128,8]{2,1,3,0:T(8,128)S(1)}, f32[2,512,128,8]{2,1,3,0:T(8,128)}, u32[]{:S(2)}) copy-start(f32[2,512,128,8]{2,1,3,0:T(8,128)} %get-tuple-element.203) | copy-start | bytes 12582916 | tf_op jit(solution)/shard_map/while
  234.9 3.4 %copy-start.1 = (f32[2,512,128,8]{2,1,3,0:T(8,128)S(1)}, f32[2,512,128,8]{2,1,3,0:T(8,128)}, u32[]{:S(2)}) copy-start(f32[2,512,128,8]{2,1,3,0:T(8,128)} %get-tuple-element.203) | copy-start | bytes 12582916 | tf_op jit(solution)/shard_map/while
  246.1 3.4 %copy-start.1 = (f32[2,512,128,8]{2,1,3,0:T(8,128)S(1)}, f32[2,512,128,8]{2,1,3,0:T(8,128)}, u32[]{:S(2)}) copy-start(f32[2,512,128,8]{2,1,3,0:T(8,128)} %get-tuple-element.203) | copy-start | bytes 12582916 | tf_op jit(solution)/shard_map/while
  257.3 3.4 %copy-start.1 = (f32[2,512,128,8]{2,1,3,0:T(8,128)S(1)}, f32[2,512,128,8]{2,1,3,0:T(8,128)}, u32[]{:S(2)}) copy-start(f32[2,512,128,8]{2,1,3,0:T(8,128)} %get-tuple-element.203) | copy-start | bytes 12582916 | tf_op jit(solution)/shard_map/while
  268.5 3.4 %copy-start.1 = (f32[2,512,128,8]{2,1,3,0:T(8,128)S(1)}, f32[2,512,128,8]{2,1,3,0:T(8,128)}, u32[]{:S(2)}) copy-start(f32[2,512,128,8]{2,1,3,0:T(8,128)} %get-tuple-element.203) | copy-start | bytes 12582916 | tf_op jit(solution)/shard_map/while
  279.7 3.4 %copy-start.1 = (f32[2,512,128,8]{2,1,3,0:T(8,128)S(1)}, f32[2,512,128,8]{2,1,3,0:T(8,128)}, u32[]{:S(2)}) copy-start(f32[2,512,128,8]{2,1,3,0:T(8,128)} %get-tuple-element.203) | copy-start | bytes 12582916 | tf_op jit(solution)/shard_map/while
  290.9 3.4 %copy-start.1 = (f32[2,512,128,8]{2,1,3,0:T(8,128)S(1)}, f32[2,512,128,8]{2,1,3,0:T(8,128)}, u32[]{:S(2)}) copy-start(f32[2,512,128,8]{2,1,3,0:T(8,128)} %get-tuple-element.203) | copy-start | bytes 12582916 | tf_op jit(solution)/shard_map/while
Sparse Core Ops, SparseCore 0:
  34.1 84.8 all-gather.2
  122.8 84.6 all-gather.4
where the time goes:
time: 311 us; the launch traced here: 310 us
  waiting for transfers between devices  124 us (40%)
  matrix products  60 us (19%)
  other arithmetic  41.4 us (13%)
  starting transfers between devices  34.9 us (11%)
  local copies, waits for them, and re-layouts  29.7 us (10%)
  between operations  14.4 us (5%)
  loops' own time  5.69 us (2%)
    all_to_all x1, waiting for transfers between devices, local(): lax.all_to_all(partials.astype(jnp.bfloat16), 'exp', split_axis=0, concat...  43 us
    all_to_all x1, waiting for transfers between devices, local(): lax.all_to_all(spread_rows, 'exp', split_axis=0, concat_axis=0, tiled=True)  36.6 us
    dot_general x8, matrix products, advance(): jnp.einsum('qhgd,khd->hgqk', grouped, key_block, preferred_element_type=j...  29.5 us
    all_to_all x1, waiting for transfers between devices, local(): lax.all_to_all(outgoing, 'ctx', split_axis=1, concat_axis=1, tiled=True)  27.4 us
    reduce_sum x8, other arithmetic, advance(): totals = totals * factor + jnp.sum(weights, axis=-1)  26.6 us
    dot_general x8, matrix products, advance(): jnp.einsum('hgqk,khd->hgqd', weights.astype(jnp.bfloat16), value_block, p...  21.1 us
    all_gather x1, waiting for transfers between devices, attention(): value_piece = lax.all_gather(value_rows, 'ctx', axis=1, tiled=True)  14.3 us
    all_to_all x1, starting transfers between devices, local(): lax.all_to_all(outgoing, 'ctx', split_axis=1, concat_axis=1, tiled=True)  13.2 us
  transfers between devices with their start and end apart: 7, of which 5 were waited for; matrix products, arithmetic and copies ran while one was open for 38% of the time, Pallas kernels for 0%

commit v1 on v0

--- a/solution.py
+++ b/solution.py
@@ -35,7 +35,10 @@
         jnp.zeros((kv_count, group_size, seq_rows, head_size), jnp.float32),
     )
     key_piece = lax.all_gather(key_rows, "ctx", axis=1, tiled=True)
-    value_piece = lax.all_gather(value_rows, "ctx", axis=1, tiled=True)
+    size = lax.axis_size("ctx")
+    blocks = jnp.stack([value_rows for _ in range(size)])
+    blocks = lax.all_to_all(blocks, "ctx", split_axis=0, concat_axis=0)
+    value_piece = jnp.concatenate(blocks, axis=1)
     piece_rows = key_piece.shape[1]
     block_rows = math.gcd(piece_rows, 512)
     block_count = piece_rows // block_rows

time: 311 us -> 344 us (1.11)
  the two profiles are of different devices: /device:TPU:16 before, /device:TPU:1 now
where the time goes in v1:
time: 344 us; the launch traced here: 343 us
  waiting for transfers between devices  116 us (34%)
  matrix products  61.4 us (18%)
  other arithmetic  42.5 us (12%)
  blocking collectives  39.7 us (12%)
  local copies, waits for them, and re-layouts  32.2 us (9%)
  starting transfers between devices  30.6 us (9%)
  between operations  14.4 us (4%)
  loops' own time  5.71 us (2%)
    all_to_all x1, waiting for transfers between devices, local(): lax.all_to_all(spread_rows, 'exp', split_axis=0, concat_axis=0, tiled=True)  48.9 us
    all_to_all x1, waiting for transfers between devices, local(): lax.all_to_all(partials.astype(jnp.bfloat16), 'exp', split_axis=0, concat...  43.2 us
    all_to_all x1, blocking collectives, local(): lax.all_to_all(outgoing, 'ctx', split_axis=1, concat_axis=1, tiled=True)  39.7 us
    dot_general x8, matrix products, advance(): jnp.einsum('qhgd,khd->hgqk', grouped, key_block, preferred_element_type=j...  29.5 us
    reduce_sum x8, other arithmetic, advance(): totals = totals * factor + jnp.sum(weights, axis=-1)  26.6 us
    all_to_all x1, waiting for transfers between devices, attention(): blocks = lax.all_to_all(blocks, 'ctx', split_axis=0, concat_axis=0)  22 us
    dot_general x8, matrix products, advance(): jnp.einsum('hgqk,khd->hgqd', weights.astype(jnp.bfloat16), value_block, p...  21.1 us
    all_to_all x1, starting transfers between devices, local(): lax.all_to_all(spread_rows, 'exp', split_axis=0, concat_axis=0, tiled=True)  10.1 us
  transfers between devices with their start and end apart: 6, of which 4 were waited for; matrix products, arithmetic and copies ran while one was open for 35% of the time, Pallas kernels for 0%

profile of v1, /device:TPU:1, one launch (start us, length us, event | category | flops | bytes accessed | tf_op | source)
XLA Modules:
  0.0 342.9 jit_solution(2159745696000030054)
XLA Ops:
  12.4 1.9 scatter_custom_fusion
  15.3 39.7 %all_to_all.25 = bf16[4,32,4,1024]{3,2,0,1:T(4,128)(2,1)S(1)} all-to-all(bf16[4,32,4,1024]{3,2,0,1:T(4,128)(2,1)S(1)} %copy.87), channel_id=1, replica_groups=mesh['ctx'=32,'exp'=16] {'ctx'}, dimensions={1} | all-to-all | bytes 2097152 | tf_op jit(solution)/shard_map/all_to_all | solution.py:124
  55.4 2.2 broadcast_in_dim.66
  57.6 10.1 %all-to-all-start.2 = ((bf16[16,16,4,1024]{3,2,1,0:T(4,128)(2,1)}), bf16[16,16,4,1024]{3,2,1,0:T(4,128)(2,1)S(1)}, u32[]{:S(2)}, u32[]{:S(2)}) async-start(bf16[16,16,4,1024]{3,2,1,0:T(4,128)(2,1)} %bitcast.120), calls=%async_computation.2 | async-start | bytes 4194304 | tf_op jit(solution)/shard_map/all_to_all | solution.py:140
  67.7 48.9 %all-to-all-done.2 = bf16[16,16,4,1024]{3,2,1,0:T(4,128)(2,1)S(1)} async-done(((bf16[16,16,4,1024]{3,2,1,0:T(4,128)(2,1)}), bf16[16,16,4,1024]{3,2,1,0:T(4,128)(2,1)S(1)}, u32[]{:S(2)}, u32[]{:S(2)}) %all-to-all-start.2) | async-done | bytes 2097184 | tf_op jit(solution)/shard_map/all_to_all | solution.py:140
  116.6 1.9 stack.10
  118.6 5.4 %all-to-all-start = ((bf16[32,1,128,2,128]{4,2,3,1,0:T(8,128)(2,1)}), bf16[32,1,128,2,128]{4,2,3,1,0:T(8,128)(2,1)S(1)}, u32[]{:S(2)}, u32[]{:S(2)}) async-start(bf16[32,1,128,2,128]{4,2,3,1,0:T(8,128)(2,1)} %stack.10), calls=%async_computation | async-start | bytes 4194304 | tf_op jit(solution)/shard_map/all_to_all | solution.py:40
  124.0 2.4 pad_maximum_fusion
  126.5 2.5 collective-permute-start
  129.6 2.1 collective-permute-done
  131.8 3.9 %maximum_select_fusion = bf16[3,384,1024]{2,1,0:T(8,128)(2,1)} fusion(bf16[1,192,1024]{2,1,0:T(8,128)(2,1)S(1)} %bitcast.125, bf16[1,192,1024]{2,1,0:T(8,128)(2,1)} %bitcast.127, bf16[1,192,1024]{2,1,0:T(8,128)(2,1)} %bitcast.129, bf16[3,192,1024]{2,1,0:T(8,128)(2,1)} %collective-permute-done, pred[]{:T(512)S(6)} %eq.35), kind=kLoop, calls=%fused_computation.30 | loop fusion | flops 20054016 | bytes 4718593 | tf_op jit(solution)/shard_map/jit(_where)/select_n | solution.py:129
  135.7 4.0 %reshape.287 = bf16[1024,1024]{1,0:T(8,128)(2,1)} reshape(bf16[16,16,4,1024]{3,2,1,0:T(4,128)(2,1)} %copy-done.2) | data formatting | bytes 4194304 | tf_op jit(solution)/shard_map/reshape | solution.py:14
  139.7 3.2 fusion.22
  142.9 3.4 multiply_convert_fusion
  146.3 2.4 dot_general.22
  148.7 4.0 %convolution_convert_fusion = bf16[16,16,4,1024]{3,1,2,0:T(8,128)(2,1)} fusion(bf16[3,384,1024]{2,1,0:T(8,128)(2,1)} %maximum_select_fusion, bf16[16,16,4,384]{3,2,1,0:T(4,128)(2,1)} %dot_general.22), kind=kOutput, calls=%fused_computation.31 | convolution fusion | flops 806354944 | bytes 3670016 | tf_op jit(solution)/shard_map/dot_general | solution.py:19
  152.7 22.0 %all-to-all-done = bf16[32,1,128,2,128]{4,2,3,1,0:T(8,128)(2,1)S(1)} async-done(((bf16[32,1,128,2,128]{4,2,3,1,0:T(8,128)(2,1)}), bf16[32,1,128,2,128]{4,2,3,1,0:T(8,128)(2,1)S(1)}, u32[]{:S(2)}, u32[]{:S(2)}) %all-to-all-start) | async-done | bytes 2097184 | tf_op jit(solution)/shard_map/all_to_all | solution.py:40
  174.7 7.4 %all-to-all-start.3 = ((bf16[16,16,4,1024]{3,1,2,0:T(8,128)(2,1)}), bf16[16,16,4,1024]{3,1,2,0:T(8,128)(2,1)}, u32[]{:S(2)}, u32[]{:S(2)}) async-start(bf16[16,16,4,1024]{3,1,2,0:T(8,128)(2,1)} %convolution_convert_fusion), calls=%async_computation.3 | async-start | bytes 4194304 | tf_op jit(solution)/shard_map/all_to_all | solution.py:142
  184.3 1.9 gather_fusion.1
  188.0 43.2 %all-to-all-done.3 = bf16[16,16,4,1024]{3,1,2,0:T(8,128)(2,1)} async-done(((bf16[16,16,4,1024]{3,1,2,0:T(8,128)(2,1)}), bf16[16,16,4,1024]{3,1,2,0:T(8,128)(2,1)}, u32[]{:S(2)}, u32[]{:S(2)}) %all-to-all-start.3) | async-done | bytes 2097184 | tf_op jit(solution)/shard_map/all_to_all | solution.py:142
  231.2 2.2 reduce
  235.3 5.1 %all-to-all-start.4 = ((bf16[4,32,4,1024]{3,2,0,1:T(4,128)(2,1)}), bf16[4,32,4,1024]{3,2,0,1:T(4,128)(2,1)S(1)}, u32[]{:S(2)}, u32[]{:S(2)}) async-start(bf16[4,32,4,1024]{3,2,0,1:T(4,128)(2,1)} %copy.91), calls=%async_computation.4 | async-start | bytes 2097152 | tf_op jit(solution)/shard_map/all_to_all | solution.py:149
  240.5 89.6 %while.15 = (s32[]{:T(128)}, f32[2,8,128]{2,1,0:T(8,128)S(1)}, f32[2,8,128]{2,1,0:T(8,128)S(1)}, f32[2,8,128,128]{3,2,1,0:T(8,128)S(1)}, s32[8]{0:T(128)S(1)}, /...) while((s32[]{:T(128)}, f32[2,8,128]{2,1,0:T(8,128)S(1)}, ...), condition=%wide.region_3.4_spmd.clone, body=%wide.region_0.3_spmd.clone.sunk | while | flops 551365248 | bytes 32904396 | solution.py:70
  241.9 3.7 %fusion.58 = (f32[2,8,128]{2,1,0:T(8,128)S(1)}, f32[2,512,128,8]{2,1,3,0:T(8,128)}) fusion(pred[128,512]{0,1:T(8,128)(4,1)S(1)} %broadcast_compare_fusion.2, bf16[128,2,8,128]{3,0,2,1:T(8,128)(2,1)S(1)} %get-tuple-element.236, bf16[8,512,2,128]{3,1,0,2:T(8,128)(2,1)} %get-tuple-element.235, s32[]{:T(128)S(6)} %copy.110), kind=kOutput, calls=%fused_computation.6.clone.1 | convolution fusion | flops 271579136 | bytes 5054468 | tf_op jit(solution)/shard_map/while/body/eval_jaxpr/qhgd,khd->hgqk/dot_general | solution.py:52
  245.6 3.3 fusion.59
  249.0 2.6 fusion.61
  253.1 3.7 %fusion.58 = (f32[2,8,128]{2,1,0:T(8,128)S(1)}, f32[2,512,128,8]{2,1,3,0:T(8,128)}) fusion(pred[128,512]{0,1:T(8,128)(4,1)S(1)} %broadcast_compare_fusion.2, bf16[128,2,8,128]{3,0,2,1:T(8,128)(2,1)S(1)} %get-tuple-element.236, bf16[8,512,2,128]{3,1,0,2:T(8,128)(2,1)} %get-tuple-element.235, s32[]{:T(128)S(6)} %copy.110), kind=kOutput, calls=%fused_computation.6.clone.1 | convolution fusion | flops 271579136 | bytes 5054468 | tf_op jit(solution)/shard_map/while/body/eval_jaxpr/qhgd,khd->hgqk/dot_general | solution.py:52
  256.8 3.3 fusion.59
  260.2 2.6 fusion.61
  264.3 3.7 %fusion.58 = (f32[2,8,128]{2,1,0:T(8,128)S(1)}, f32[2,512,128,8]{2,1,3,0:T(8,128)}) fusion(pred[128,512]{0,1:T(8,128)(4,1)S(1)} %broadcast_compare_fusion.2, bf16[128,2,8,128]{3,0,2,1:T(8,128)(2,1)S(1)} %get-tuple-element.236, bf16[8,512,2,128]{3,1,0,2:T(8,128)(2,1)} %get-tuple-element.235, s32[]{:T(128)S(6)} %copy.110), kind=kOutput, calls=%fused_computation.6.clone.1 | convolution fusion | flops 271579136 | bytes 5054468 | tf_op jit(solution)/shard_map/while/body/eval_jaxpr/qhgd,khd->hgqk/dot_general | solution.py:52
  268.0 3.3 fusion.59
  271.4 2.6 fusion.61
  275.5 3.7 %fusion.58 = (f32[2,8,128]{2,1,0:T(8,128)S(1)}, f32[2,512,128,8]{2,1,3,0:T(8,128)}) fusion(pred[128,512]{0,1:T(8,128)(4,1)S(1)} %broadcast_compare_fusion.2, bf16[128,2,8,128]{3,0,2,1:T(8,128)(2,1)S(1)} %get-tuple-element.236, bf16[8,512,2,128]{3,1,0,2:T(8,128)(2,1)} %get-tuple-element.235, s32[]{:T(128)S(6)} %copy.110), kind=kOutput, calls=%fused_computation.6.clone.1 | convolution fusion | flops 271579136 | bytes 5054468 | tf_op jit(solution)/shard_map/while/body/eval_jaxpr/qhgd,khd->hgqk/dot_general | solution.py:52
  279.2 3.3 fusion.59
  282.6 2.6 fusion.61
  286.7 3.7 %fusion.58 = (f32[2,8,128]{2,1,0:T(8,128)S(1)}, f32[2,512,128,8]{2,1,3,0:T(8,128)}) fusion(pred[128,512]{0,1:T(8,128)(4,1)S(1)} %broadcast_compare_fusion.2, bf16[128,2,8,128]{3,0,2,1:T(8,128)(2,1)S(1)} %get-tuple-element.236, bf16[8,512,2,128]{3,1,0,2:T(8,128)(2,1)} %get-tuple-element.235, s32[]{:T(128)S(6)} %copy.110), kind=kOutput, calls=%fused_computation.6.clone.1 | convolution fusion | flops 271579136 | bytes 5054468 | tf_op jit(solution)/shard_map/while/body/eval_jaxpr/qhgd,khd->hgqk/dot_general | solution.py:52
  290.4 3.3 fusion.59
  293.8 2.6 fusion.61
  297.9 3.7 %fusion.58 = (f32[2,8,128]{2,1,0:T(8,128)S(1)}, f32[2,512,128,8]{2,1,3,0:T(8,128)}) fusion(pred[128,512]{0,1:T(8,128)(4,1)S(1)} %broadcast_compare_fusion.2, bf16[128,2,8,128]{3,0,2,1:T(8,128)(2,1)S(1)} %get-tuple-element.236, bf16[8,512,2,128]{3,1,0,2:T(8,128)(2,1)} %get-tuple-element.235, s32[]{:T(128)S(6)} %copy.110), kind=kOutput, calls=%fused_computation.6.clone.1 | convolution fusion | flops 271579136 | bytes 5054468 | tf_op jit(solution)/shard_map/while/body/eval_jaxpr/qhgd,khd->hgqk/dot_general | solution.py:52
  301.6 3.3 fusion.59
  305.1 2.6 fusion.61
  309.1 3.7 %fusion.58 = (f32[2,8,128]{2,1,0:T(8,128)S(1)}, f32[2,512,128,8]{2,1,3,0:T(8,128)}) fusion(pred[128,512]{0,1:T(8,128)(4,1)S(1)} %broadcast_compare_fusion.2, bf16[128,2,8,128]{3,0,2,1:T(8,128)(2,1)S(1)} %get-tuple-element.236, bf16[8,512,2,128]{3,1,0,2:T(8,128)(2,1)} %get-tuple-element.235, s32[]{:T(128)S(6)} %copy.110), kind=kOutput, calls=%fused_computation.6.clone.1 | convolution fusion | flops 271579136 | bytes 5054468 | tf_op jit(solution)/shard_map/while/body/eval_jaxpr/qhgd,khd->hgqk/dot_general | solution.py:52
  312.8 3.3 fusion.59
  316.3 2.6 fusion.61
  320.3 3.7 %fusion.58 = (f32[2,8,128]{2,1,0:T(8,128)S(1)}, f32[2,512,128,8]{2,1,3,0:T(8,128)}) fusion(pred[128,512]{0,1:T(8,128)(4,1)S(1)} %broadcast_compare_fusion.2, bf16[128,2,8,128]{3,0,2,1:T(8,128)(2,1)S(1)} %get-tuple-element.236, bf16[8,512,2,128]{3,1,0,2:T(8,128)(2,1)} %get-tuple-element.235, s32[]{:T(128)S(6)} %copy.110), kind=kOutput, calls=%fused_computation.6.clone.1 | convolution fusion | flops 271579136 | bytes 5054468 | tf_op jit(solution)/shard_map/while/body/eval_jaxpr/qhgd,khd->hgqk/dot_general | solution.py:52
  324.0 3.3 fusion.59
  327.5 2.6 fusion.61
  333.7 2.3 multiply_reduce_fusion
  (144 shorter events, 23.2 us)
Async XLA Ops:
  7.2 176.9 %copy-start = (bf16[1024,128]{1,0:T(8,128)(2,1)S(1)}, bf16[1024,128]{1,0:T(8,128)(2,1)}, u32[]{:S(2)}) copy-start(bf16[1024,128]{1,0:T(8,128)(2,1)} %param.18) | copy-start | bytes 786436
  57.6 10.1 %copy-start.6 = (bf16[1,128,2,128]{3,2,1,0:T(2,128)(2,1)S(1)}, bf16[1,128,2,128]{3,2,1,0:T(2,128)(2,1)}, u32[]{:S(2)}) copy-start(bf16[1,128,2,128]{3,2,1,0:T(2,128)(2,1)} %param.15) | copy-start | bytes 196612
  57.6 59.0 %all-to-all-start.2 = ((bf16[16,16,4,1024]{3,2,1,0:T(4,128)(2,1)}), bf16[16,16,4,1024]{3,2,1,0:T(4,128)(2,1)S(1)}, u32[]{:S(2)}, u32[]{:S(2)}) async-start(bf16[16,16,4,1024]{3,2,1,0:T(4,128)(2,1)} %bitcast.120), calls=%async_computation.2 | async-start | bytes 4194304 | tf_op jit(solution)/shard_map/all_to_all | solution.py:140
  116.6 2.0 copy-start.2
  118.6 10.4 %copy-start.7 = (bf16[1,128,2,128]{3,2,1,0:T(2,128)(2,1)S(1)}, bf16[1,128,2,128]{3,2,1,0:T(2,128)(2,1)}, u32[]{:S(2)}) copy-start(bf16[1,128,2,128]{3,2,1,0:T(2,128)(2,1)} %param.14) | copy-start | bytes 196612
  118.6 56.1 %all-to-all-start = ((bf16[32,1,128,2,128]{4,2,3,1,0:T(8,128)(2,1)}), bf16[32,1,128,2,128]{4,2,3,1,0:T(8,128)(2,1)S(1)}, u32[]{:S(2)}, u32[]{:S(2)}) async-start(bf16[32,1,128,2,128]{4,2,3,1,0:T(8,128)(2,1)} %stack.10), calls=%async_computation | async-start | bytes 4194304 | tf_op jit(solution)/shard_map/all_to_all | solution.py:40
  124.0 7.8 %copy-start.4 = (bf16[192,1024]{1,0:T(8,128)(2,1)S(1)}, bf16[192,1024]{1,0:T(8,128)(2,1)}, u32[]{:S(2)}) copy-start(bf16[192,1024]{1,0:T(8,128)(2,1)} %param.21) | copy-start | bytes 1179652
  124.0 116.5 %all-gather.2.cloned.1.call-start = ((), (), s32[]{:S(2)}) async-start(), calls=%async_computation.5 | async-start | bytes 2162688 | tf_op jit(solution)/shard_map/all_gather | solution.py:37
  126.5 5.3 %collective-permute-start = (bf16[3,192,1024]{2,1,0:T(8,128)(2,1)}, bf16[3,192,1024]{2,1,0:T(8,128)(2,1)}, u32[]{:S(2)}, u32[]{:S(2)}) collective-permute-start(bf16[3,192,1024]{2,1,0:T(8,128)(2,1)} %pad_maximum_fusion), channel_id=1, source_target_pairs={{0,1},{1,0},{2,3},{3,2},{4,5},{5,4},{6,7},{7,6},{8,9},{9,8},{10,11... | collective-permute-start | bytes 3538952 | tf_op jit(solution)/shard_map/ppermute | solution.py:9
  139.7 3.2 copy-start.3
  152.7 30.9 %copy-start.8 = (s32[1,128,2]{1,2,0:T(2,128)S(1)}, s32[1,128,2]{1,2,0:T(2,128)}, u32[]{:S(2)}) copy-start(s32[1,128,2]{1,2,0:T(2,128)} %param.16) | copy-start | bytes 3076
  174.7 56.5 %all-to-all-start.3 = ((bf16[16,16,4,1024]{3,1,2,0:T(8,128)(2,1)}), bf16[16,16,4,1024]{3,1,2,0:T(8,128)(2,1)}, u32[]{:S(2)}, u32[]{:S(2)}) async-start(bf16[16,16,4,1024]{3,1,2,0:T(8,128)(2,1)} %convolution_convert_fusion), calls=%async_computation.3 | async-start | bytes 4194304 | tf_op jit(solution)/shard_map/all_to_all | solution.py:142
  233.5 6.9 %copy-start.5 = (f32[2,8,128,128]{3,2,1,0:T(8,128)S(1)}, f32[2,8,128,128]{3,2,1,0:T(8,128)}, u32[]{:S(2)}) copy-start(f32[2,8,128,128]{3,2,1,0:T(8,128)} %custom-call.4) | copy-start | bytes 3145732
  235.3 96.3 %all-to-all-start.4 = ((bf16[4,32,4,1024]{3,2,0,1:T(4,128)(2,1)}), bf16[4,32,4,1024]{3,2,0,1:T(4,128)(2,1)S(1)}, u32[]{:S(2)}, u32[]{:S(2)}) async-start(bf16[4,32,4,1024]{3,2,0,1:T(4,128)(2,1)} %copy.91), calls=%async_computation.4 | async-start | bytes 2097152 | tf_op jit(solution)/shard_map/all_to_all | solution.py:149
  245.6 3.4 %copy-start.1 = (f32[2,512,128,8]{2,1,3,0:T(8,128)S(1)}, f32[2,512,128,8]{2,1,3,0:T(8,128)}, u32[]{:S(2)}) copy-start(f32[2,512,128,8]{2,1,3,0:T(8,128)} %get-tuple-element.203) | copy-start | bytes 12582916 | tf_op jit(solution)/shard_map/while
  256.8 3.4 %copy-start.1 = (f32[2,512,128,8]{2,1,3,0:T(8,128)S(1)}, f32[2,512,128,8]{2,1,3,0:T(8,128)}, u32[]{:S(2)}) copy-start(f32[2,512,128,8]{2,1,3,0:T(8,128)} %get-tuple-element.203) | copy-start | bytes 12582916 | tf_op jit(solution)/shard_map/while
  268.0 3.4 %copy-start.1 = (f32[2,512,128,8]{2,1,3,0:T(8,128)S(1)}, f32[2,512,128,8]{2,1,3,0:T(8,128)}, u32[]{:S(2)}) copy-start(f32[2,512,128,8]{2,1,3,0:T(8,128)} %get-tuple-element.203) | copy-start | bytes 12582916 | tf_op jit(solution)/shard_map/while
  279.2 3.4 %copy-start.1 = (f32[2,512,128,8]{2,1,3,0:T(8,128)S(1)}, f32[2,512,128,8]{2,1,3,0:T(8,128)}, u32[]{:S(2)}) copy-start(f32[2,512,128,8]{2,1,3,0:T(8,128)} %get-tuple-element.203) | copy-start | bytes 12582916 | tf_op jit(solution)/shard_map/while
  290.4 3.4 %copy-start.1 = (f32[2,512,128,8]{2,1,3,0:T(8,128)S(1)}, f32[2,512,128,8]{2,1,3,0:T(8,128)}, u32[]{:S(2)}) copy-start(f32[2,512,128,8]{2,1,3,0:T(8,128)} %get-tuple-element.203) | copy-start | bytes 12582916 | tf_op jit(solution)/shard_map/while
  301.6 3.4 %copy-start.1 = (f32[2,512,128,8]{2,1,3,0:T(8,128)S(1)}, f32[2,512,128,8]{2,1,3,0:T(8,128)}, u32[]{:S(2)}) copy-start(f32[2,512,128,8]{2,1,3,0:T(8,128)} %get-tuple-element.203) | copy-start | bytes 12582916 | tf_op jit(solution)/shard_map/while
  312.8 3.4 %copy-start.1 = (f32[2,512,128,8]{2,1,3,0:T(8,128)S(1)}, f32[2,512,128,8]{2,1,3,0:T(8,128)}, u32[]{:S(2)}) copy-start(f32[2,512,128,8]{2,1,3,0:T(8,128)} %get-tuple-element.203) | copy-start | bytes 12582916 | tf_op jit(solution)/shard_map/while
  324.0 3.4 %copy-start.1 = (f32[2,512,128,8]{2,1,3,0:T(8,128)S(1)}, f32[2,512,128,8]{2,1,3,0:T(8,128)}, u32[]{:S(2)}) copy-start(f32[2,512,128,8]{2,1,3,0:T(8,128)} %get-tuple-element.203) | copy-start | bytes 12582916 | tf_op jit(solution)/shard_map/while
Sparse Core Ops, SparseCore 0:
  129.8 85.6 all-gather.1
